TPU v7x, 512 devices: a whole 4x4x16 slice. The times are simulated.
512 devices in a mesh: ctx: 64 (over z, y_hi, core), head: 8 (over y_lo, x).
Axes of the slice: x: 4, y: 4 (y_hi: 2, y_lo: 2; y = y_hi * 2 + y_lo), z: 16, core: 2. Of those that a mesh axis runs over, the one named last changes fastest.
Arguments:
- query_states: bfloat16 [32768, 8192], P('ctx', 'head'), may hold values from -5 to 5
- key_states: bfloat16 [32768, 1024], P('ctx', 'head'), may hold values from -5 to 5
- value_states: bfloat16 [32768, 1024], P('ctx', 'head'), may hold values from -6 to 6
- out_grad: bfloat16 [32768, 8192], P('ctx', 'head'), may hold values from -6 to 6
- block_lists: int32 [256, 4], replicated, may hold values from 0 to 255, as said below
Outputs:
- query_grad: bfloat16 [32768, 8192], P(('ctx', 'head'))
- key_grad: bfloat16 [32768, 1024], P(('ctx', 'head'))
- value_grad: bfloat16 [32768, 1024], P(('ctx', 'head'))
Inputs may be any that keep to these rules, and one draw needn't show every extreme that they name: `block_lists`: entry 0 of row b is b. The other entries name distinct blocks below b, each held by the same index of ctx as b or by one of the 8 indices just below it; a row with fewer candidates repeats b in its remaining entries. Taken over the 4 rows of one index of ctx, the listed blocks that another index of ctx holds are at most one distinct block.
All inputs are finite; a program needn't handle non-finite values.
Results may differ from a plain program's by a relative error of at most 0.012.
Values may be sent and summed in bfloat16 or wider, within the bound.
No kernel may reach another device: no remote copies, remote signals or barrier semaphores. Data moves between devices by JAX's collectives and lax.ppermute only.
A program may use at most 64 MiB of HBM per device.

v0:
```python
import math
import jax
import jax.numpy as jnp
from jax import lax
from jax.sharding import PartitionSpec as P

HEADS = 64
KV_HEADS = 8
HEAD_DIM = 128
BLOCK = 128
REACH = 8


def from_behind(x, axis, by):
    devices = lax.axis_size(axis)
    pairs = [(i, i + by) for i in range(devices) if 0 <= i + by < devices]
    return lax.ppermute(x, axis, pairs)


def block_grads(query_blk, grad_blk, kv_blk, entries, block_ids):
    kv_cols = kv_blk.shape[-1] // 2
    kv_heads = kv_cols // HEAD_DIM
    leading = kv_blk.shape[:3]
    scaling = 1.0 / math.sqrt(HEAD_DIM)
    key_blk = kv_blk[..., :kv_cols].reshape(leading + (kv_heads, HEAD_DIM))
    value_blk = kv_blk[..., kv_cols:].reshape(leading + (kv_heads, HEAD_DIM))
    chosen = entries.shape[1]
    order_ids = jnp.arange(chosen, dtype=jnp.int32)
    repeat = (entries[:, :, None] == entries[:, None, :]) & (
        order_ids[None, None, :] < order_ids[None, :, None]
    )
    usable = jnp.logical_not(jnp.any(repeat, axis=2))
    positions = jnp.arange(BLOCK, dtype=jnp.int32)
    causal = positions[None, :] <= positions[:, None]
    earlier = entries < block_ids[:, None]
    allowed = usable[:, None, :, None] & (earlier[:, None, :, None] | causal[None, :, None, :])
    allowed = allowed[:, None, None]
    scores = (
        jnp.einsum("nighd,netgd->nghiet", query_blk, key_blk, preferred_element_type=jnp.float32)
        * scaling
    )
    scores = jnp.where(allowed, scores, -1e30)
    row_max = jnp.max(scores, axis=(4, 5), keepdims=True)
    total = jnp.sum(jnp.where(allowed, jnp.exp(scores - row_max), 0.0), axis=(4, 5), keepdims=True)
    log_total = row_max + jnp.log(total)
    prob = jnp.where(allowed, jnp.exp(scores - log_total), 0.0)
    prob_half = prob.astype(jnp.bfloat16)
    output = jnp.einsum(
        "nghiet,netgd->nighd", prob_half, value_blk, preferred_element_type=jnp.float32
    ).astype(jnp.bfloat16)
    output_wide = lax.optimization_barrier(output).astype(jnp.float32)
    row_dot = jnp.sum(grad_blk.astype(jnp.float32) * output_wide, axis=-1)
    prob_grad = jnp.einsum(
        "nighd,netgd->nghiet", grad_blk, value_blk, preferred_element_type=jnp.float32
    )
    centred = prob_grad - jnp.transpose(row_dot, (0, 2, 3, 1))[..., None, None]
    score_grad = (prob * centred * scaling).astype(jnp.bfloat16)
    block_qgrad = jnp.einsum(
        "nghiet,netgd->nighd", score_grad, key_blk, preferred_element_type=jnp.float32
    ).astype(jnp.bfloat16)
    key_part = jnp.einsum(
        "nghiet,nighd->netgd", score_grad, query_blk, preferred_element_type=jnp.float32
    )
    value_part = jnp.einsum(
        "nghiet,nighd->netgd", prob_half, grad_blk, preferred_element_type=jnp.float32
    )
    pair_terms = jnp.concatenate(
        [key_part.reshape(leading + (kv_cols,)), value_part.reshape(leading + (kv_cols,))], axis=-1
    )
    return (block_qgrad, pair_terms)


def fetch_block(outgoing_one, distance):
    return from_behind(outgoing_one, "ctx", distance)


def return_block(terms_one, distance):
    return from_behind(terms_one.astype(jnp.bfloat16), "ctx", -distance).astype(terms_one.dtype)


def body(query_states, key_states, value_states, out_grad, block_lists):
    ctx_count = lax.axis_size("ctx")
    myself = lax.axis_index("ctx")
    tok_rows = query_states.shape[0]
    kv_cols = key_states.shape[1]
    kv_heads = kv_cols // HEAD_DIM
    group_size = HEADS // KV_HEADS
    blocks_here = tok_rows // BLOCK
    chosen = block_lists.shape[1]
    lists_by_dev = block_lists.reshape(ctx_count, blocks_here * chosen)
    slot_ids = jnp.arange(blocks_here, dtype=jnp.int32)
    distances = jnp.arange(1, REACH + 1, dtype=jnp.int32)
    targets = myself + distances
    target_ok = targets < ctx_count
    target_rows = jnp.take(lists_by_dev, jnp.minimum(targets, ctx_count - 1), axis=0)
    mine = target_rows // blocks_here == myself
    requested = jnp.max(jnp.where(mine, target_rows % blocks_here, -1), axis=1)
    requested = jnp.where(target_ok, requested, -1)
    kv_local = jnp.concatenate([key_states, value_states], axis=1).reshape(
        blocks_here, BLOCK, 2 * kv_cols
    )
    pick_rows = (requested[:, None] == slot_ids[None, :]).astype(jnp.bfloat16)
    outgoing = jnp.einsum(
        "sj,jtc->stc", pick_rows, kv_local, preferred_element_type=jnp.float32
    ).astype(jnp.bfloat16)
    arrivals = []
    for distance in range(1, REACH + 1):
        arrivals.append(fetch_block(outgoing[distance - 1], distance))
    incoming = jnp.stack(arrivals, axis=0)
    own_entries = lax.dynamic_slice_in_dim(block_lists, myself * blocks_here, blocks_here, 0)
    flat_entries = own_entries.reshape(blocks_here * chosen)
    behind = myself - flat_entries // blocks_here
    at_home = behind == 0
    source_row = jnp.where(at_home, REACH + flat_entries % blocks_here, behind - 1)
    kv_stock = jnp.concatenate([incoming, kv_local], axis=0)
    gathered = jnp.take(kv_stock, source_row, axis=0).reshape(
        blocks_here, chosen, BLOCK, 2 * kv_cols
    )
    per_step = 1
    step_count = blocks_here // per_step
    query_steps = query_states.reshape(step_count, per_step, BLOCK, kv_heads, group_size, HEAD_DIM)
    grad_steps = out_grad.reshape(step_count, per_step, BLOCK, kv_heads, group_size, HEAD_DIM)
    kv_steps = gathered.reshape(step_count, per_step, chosen, BLOCK, 2 * kv_cols)
    entry_steps = own_entries.reshape(step_count, per_step, chosen)
    block_steps = (myself * blocks_here + slot_ids).reshape(step_count, per_step)

    def one_step(pieces):
        return block_grads(pieces[0], pieces[1], pieces[2], pieces[3], pieces[4])

    qgrad_steps, pair_steps = lax.map(
        one_step, (query_steps, grad_steps, kv_steps, entry_steps, block_steps)
    )
    query_local = qgrad_steps.reshape(tok_rows, kv_heads * group_size * HEAD_DIM)
    pair_terms = pair_steps.reshape(blocks_here * chosen, BLOCK, 2 * kv_cols)
    keep_home = (
        at_home[None, :] & ((flat_entries % blocks_here)[None, :] == slot_ids[:, None])
    ).astype(jnp.float32)
    totals = jnp.einsum("jp,ptc->jtc", keep_home, pair_terms, precision=lax.Precision.HIGHEST)
    by_distance = behind[None, :] == distances[:, None]
    sendback = jnp.einsum(
        "sp,ptc->stc", by_distance.astype(jnp.float32), pair_terms, precision=lax.Precision.HIGHEST
    )
    returned = []
    for distance in range(1, REACH + 1):
        returned.append(return_block(sendback[distance - 1], distance))
    arrived = jnp.stack(returned, axis=0)
    credit = (requested[None, :] == slot_ids[:, None]).astype(jnp.float32)
    totals = totals + jnp.einsum("js,stc->jtc", credit, arrived, precision=lax.Precision.HIGHEST)
    key_local = totals[..., :kv_cols].reshape(tok_rows, kv_cols).astype(jnp.bfloat16)
    value_local = totals[..., kv_cols:].reshape(tok_rows, kv_cols).astype(jnp.bfloat16)
    query_grad, key_grad, value_grad = (
        lax.all_to_all(query_local, "head", split_axis=0, concat_axis=1, tiled=True),
        lax.all_to_all(key_local, "head", split_axis=0, concat_axis=1, tiled=True),
        lax.all_to_all(value_local, "head", split_axis=0, concat_axis=1, tiled=True),
    )
    return (query_grad, key_grad, value_grad)


def solution(mesh):
    in_specs = (P("ctx", "head"), P("ctx", "head"), P("ctx", "head"), P("ctx", "head"), P())
    out_specs = (P(("ctx", "head"), None), P(("ctx", "head"), None), P(("ctx", "head"), None))
    return jax.shard_map(body, mesh=mesh, in_specs=in_specs, out_specs=out_specs, check_vma=False)
```

profile of v0, /device:TPU:64, one launch (start us, length us, event | category | flops | bytes accessed | tf_op | source)
XLA Modules:
  0.0 164.2 jit_solution(14954413630219802681)
XLA Ops:
  0.7 0.8 copy.328
  2.4 1.0 pad_maximum_fusion
  3.8 0.9 fusion.55
  5.4 1.9 %collective-permute-start = (bf16[128,256]{1,0:T(8,128)(2,1)}, bf16[128,256]{1,0:T(8,128)(2,1)}, u32[]{:S(2)}, u32[]{:S(2)}) collective-permute-start(bf16[128,256]{1,0:T(8,128)(2,1)} %bitcast.256), channel_id=1, source_target_pairs={{0,8},{8,16},{16,24},{24,32},{32,40},{40,48},{48,56},{56,64},{64,7... | collective-permute-start | bytes 196616 | tf_op jit(solution)/shard_map/ppermute | solution.py:17
  7.9 5.1 %collective-permute-start.1 = (bf16[128,256]{1,0:T(8,128)(2,1)}, bf16[128,256]{1,0:T(8,128)(2,1)}, u32[]{:S(2)}, u32[]{:S(2)}) collective-permute-start(bf16[128,256]{1,0:T(8,128)(2,1)} %bitcast.255), channel_id=1, source_target_pairs={{0,16},{8,24},{16,32},{24,40},{32,48},{40,56},{48,64},{56,72},{64,... | collective-permute-start | bytes 196616 | tf_op jit(solution)/shard_map/ppermute | solution.py:17
  13.7 6.2 %collective-permute-start.2 = (bf16[128,256]{1,0:T(8,128)(2,1)}, bf16[128,256]{1,0:T(8,128)(2,1)}, u32[]{:S(2)}, u32[]{:S(2)}) collective-permute-start(bf16[128,256]{1,0:T(8,128)(2,1)} %bitcast.254), channel_id=1, source_target_pairs={{0,24},{8,32},{16,40},{24,48},{32,56},{40,64},{48,72},{56,80},{64,... | collective-permute-start | bytes 196616 | tf_op jit(solution)/shard_map/ppermute | solution.py:17
  19.9 5.0 %collective-permute-start.3 = (bf16[128,256]{1,0:T(8,128)(2,1)S(1)}, bf16[128,256]{1,0:T(8,128)(2,1)}, u32[]{:S(2)}, u32[]{:S(2)}) collective-permute-start(bf16[128,256]{1,0:T(8,128)(2,1)S(1)} %bitcast.319), channel_id=1, source_target_pairs={{0,32},{8,40},{16,48},{24,56},{32,64},{40,72},{48,80},{56,88},{64,... | collective-permute-start | bytes 196616 | tf_op jit(solution)/shard_map/ppermute | solution.py:17
  25.0 1.9 %collective-permute-start.4 = (bf16[128,256]{1,0:T(8,128)(2,1)S(1)}, bf16[128,256]{1,0:T(8,128)(2,1)}, u32[]{:S(2)}, u32[]{:S(2)}) collective-permute-start(bf16[128,256]{1,0:T(8,128)(2,1)S(1)} %bitcast.318), channel_id=1, source_target_pairs={{0,40},{8,48},{16,56},{24,64},{32,72},{40,80},{48,88},{56,96},{64,... | collective-permute-start | bytes 196616 | tf_op jit(solution)/shard_map/ppermute | solution.py:17
  29.0 1.3 copy.400
  30.8 4.9 %collective-permute-start.5 = (bf16[128,256]{1,0:T(8,128)(2,1)S(1)}, bf16[128,256]{1,0:T(8,128)(2,1)S(1)}, u32[]{:S(2)}, u32[]{:S(2)}) collective-permute-start(bf16[128,256]{1,0:T(8,128)(2,1)S(1)} %bitcast.330), channel_id=1, source_target_pairs={{0,48},{8,56},{16,64},{24,72},{32,80},{40,88},{48,96},{56,104},{64... | collective-permute-start | bytes 196616 | tf_op jit(solution)/shard_map/ppermute | solution.py:17
  35.8 0.8 bitcast_dynamic-update-slice_fusion.7
  36.6 9.2 %collective-permute-start.6 = (bf16[128,256]{1,0:T(8,128)(2,1)S(1)}, bf16[128,256]{1,0:T(8,128)(2,1)S(1)}, u32[]{:S(2)}, u32[]{:S(2)}) collective-permute-start(bf16[128,256]{1,0:T(8,128)(2,1)S(1)} %bitcast.324), channel_id=1, source_target_pairs={{0,56},{8,64},{16,72},{24,80},{32,88},{40,96},{48,104},{56,112},{6... | collective-permute-start | bytes 196616 | tf_op jit(solution)/shard_map/ppermute | solution.py:17
  45.8 0.8 bitcast_dynamic-update-slice_fusion.6
  46.7 3.4 %collective-permute-start.7 = (bf16[128,256]{1,0:T(8,128)(2,1)S(1)}, bf16[128,256]{1,0:T(8,128)(2,1)S(1)}, u32[]{:S(2)}, u32[]{:S(2)}) collective-permute-start(bf16[128,256]{1,0:T(8,128)(2,1)S(1)} %bitcast.321), channel_id=1, source_target_pairs={{0,64},{8,72},{16,80},{24,88},{32,96},{40,104},{48,112},{56,120},{... | collective-permute-start | bytes 196616 | tf_op jit(solution)/shard_map/ppermute | solution.py:17
  50.1 0.8 bitcast_dynamic-update-slice_fusion.5
  50.9 0.8 bitcast_dynamic-update-slice_fusion.4
  51.8 0.8 bitcast_dynamic-update-slice_fusion.3
  52.7 1.2 collective-permute-done.7
  54.7 32.7 %while.12 = (s32[]{:T(128)}, bf16[4,1,128,1,8,128]{5,4,2,0,3,1:T(8,128)(2,1)}, f32[4,1,4,128,256]{3,4,2,1,0:T(8,128)}, bf16[4,1,4,128,256]{4,3,2,1,0:T(8,128)(2,...) while((s32[]{:T(128)}, ...), condition=%wide.region_6.7_spmd, body=%wide.region_1.6_spmd.sunk | while | flops 815806528 | bytes 21442768 | solution.py:130
  55.3 0.7 broadcast_compare_fusion.3
  56.3 1.0 constant_dynamic-slice_fusion.8
  59.5 0.7 fusion.85
  61.3 0.7 constant_dynamic-update-slice_fusion.3
  62.0 0.9 fusion.87
  64.5 1.0 constant_dynamic-slice_fusion.8
  67.7 0.7 fusion.85
  69.5 0.7 constant_dynamic-update-slice_fusion.3
  70.2 0.8 fusion.87
  72.7 1.0 constant_dynamic-slice_fusion.8
  75.9 0.7 fusion.85
  77.7 0.7 constant_dynamic-update-slice_fusion.3
  78.4 0.8 fusion.87
  80.8 1.0 constant_dynamic-slice_fusion.8
  84.1 0.7 fusion.85
  85.8 0.7 constant_dynamic-update-slice_fusion.3
  86.6 0.8 fusion.87
  87.4 2.2 %copy.339 = f32[16,128,256]{2,0,1:T(8,128)S(1)} copy(f32[16,128,256]{1,2,0:T(8,128)} %bitcast.313) | data formatting | bytes 4194304 | tf_op jit(solution)/shard_map/reshape | solution.py:134
  89.7 0.8 convolution_convert_fusion.1
  90.5 0.9 fusion.54
  91.5 1.9 %collective-permute-start.8 = (bf16[128,256]{1,0:T(8,128)(2,1)S(1)}, bf16[128,256]{1,0:T(8,128)(2,1)S(1)}, u32[]{:S(2)}, u32[]{:S(2)}) collective-permute-start(bf16[128,256]{1,0:T(8,128)(2,1)S(1)} %bitcast.338), channel_id=1, source_target_pairs={{8,0},{16,8},{24,16},{32,24},{40,32},{48,40},{56,48},{64,56},{72,6... | collective-permute-start | bytes 196616 | tf_op jit(solution)/shard_map/ppermute | solution.py:17
  93.4 4.4 %collective-permute-start.9 = (bf16[128,256]{1,0:T(8,128)(2,1)S(1)}, bf16[128,256]{1,0:T(8,128)(2,1)S(1)}, u32[]{:S(2)}, u32[]{:S(2)}) collective-permute-start(bf16[128,256]{1,0:T(8,128)(2,1)S(1)} %bitcast.332), channel_id=1, source_target_pairs={{16,0},{24,8},{32,16},{40,24},{48,32},{56,40},{64,48},{72,56},{80,... | collective-permute-start | bytes 196616 | tf_op jit(solution)/shard_map/ppermute | solution.py:17
  97.8 2.7 %collective-permute-start.10 = (bf16[128,256]{1,0:T(8,128)(2,1)S(1)}, bf16[128,256]{1,0:T(8,128)(2,1)S(1)}, u32[]{:S(2)}, u32[]{:S(2)}) collective-permute-start(bf16[128,256]{1,0:T(8,128)(2,1)S(1)} %bitcast.328), channel_id=1, source_target_pairs={{24,0},{32,8},{40,16},{48,24},{56,32},{64,40},{72,48},{80,56},{88,... | collective-permute-start | bytes 196616 | tf_op jit(solution)/shard_map/ppermute | solution.py:17
  100.7 2.1 %collective-permute-start.11 = (bf16[128,256]{1,0:T(8,128)(2,1)S(1)}, bf16[128,256]{1,0:T(8,128)(2,1)S(1)}, u32[]{:S(2)}, u32[]{:S(2)}) collective-permute-start(bf16[128,256]{1,0:T(8,128)(2,1)S(1)} %bitcast.333), channel_id=1, source_target_pairs={{32,0},{40,8},{48,16},{56,24},{64,32},{72,40},{80,48},{88,56},{96,... | collective-permute-start | bytes 196616 | tf_op jit(solution)/shard_map/ppermute | solution.py:17
  102.8 1.9 %collective-permute-start.12 = (bf16[128,256]{1,0:T(8,128)(2,1)S(1)}, bf16[128,256]{1,0:T(8,128)(2,1)S(1)}, u32[]{:S(2)}, u32[]{:S(2)}) collective-permute-start(bf16[128,256]{1,0:T(8,128)(2,1)S(1)} %bitcast.329), channel_id=1, source_target_pairs={{40,0},{48,8},{56,16},{64,24},{72,32},{80,40},{88,48},{96,56},{104... | collective-permute-start | bytes 196616 | tf_op jit(solution)/shard_map/ppermute | solution.py:17
  104.7 1.9 %collective-permute-start.13 = (bf16[128,256]{1,0:T(8,128)(2,1)S(1)}, bf16[128,256]{1,0:T(8,128)(2,1)S(1)}, u32[]{:S(2)}, u32[]{:S(2)}) collective-permute-start(bf16[128,256]{1,0:T(8,128)(2,1)S(1)} %bitcast.323), channel_id=1, source_target_pairs={{48,0},{56,8},{64,16},{72,24},{80,32},{88,40},{96,48},{104,56},{11... | collective-permute-start | bytes 196616 | tf_op jit(solution)/shard_map/ppermute | solution.py:17
  106.7 1.9 %collective-permute-start.14 = (bf16[128,256]{1,0:T(8,128)(2,1)S(1)}, bf16[128,256]{1,0:T(8,128)(2,1)S(1)}, u32[]{:S(2)}, u32[]{:S(2)}) collective-permute-start(bf16[128,256]{1,0:T(8,128)(2,1)S(1)} %bitcast.322), channel_id=1, source_target_pairs={{56,0},{64,8},{72,16},{80,24},{88,32},{96,40},{104,48},{112,56},{1... | collective-permute-start | bytes 196616 | tf_op jit(solution)/shard_map/ppermute | solution.py:17
  108.6 2.1 %collective-permute-start.15 = (bf16[128,256]{1,0:T(8,128)(2,1)S(1)}, bf16[128,256]{1,0:T(8,128)(2,1)S(1)}, u32[]{:S(2)}, u32[]{:S(2)}) collective-permute-start(bf16[128,256]{1,0:T(8,128)(2,1)S(1)} %bitcast.320), channel_id=1, source_target_pairs={{64,0},{72,8},{80,16},{88,24},{96,32},{104,40},{112,48},{120,56},{... | collective-permute-start | bytes 196616 | tf_op jit(solution)/shard_map/ppermute | solution.py:17
  110.7 0.8 fusion.39
  112.1 1.1 collective-permute-done.13
  113.4 1.4 collective-permute-done.14
  114.9 7.6 %collective-permute-done.15 = bf16[128,256]{1,0:T(8,128)(2,1)S(1)} collective-permute-done((bf16[128,256]{1,0:T(8,128)(2,1)S(1)}, bf16[128,256]{1,0:T(8,128)(2,1)S(1)}, u32[]{:S(2)}, u32[]{:S(2)}) %collective-permute-start.15) | collective-permute-done | bytes 65568 | tf_op jit(solution)/shard_map/ppermute | solution.py:17
  122.6 1.6 stack.78
  124.6 0.7 copy.351
  125.3 4.4 %all-to-all-start.2 = ((bf16[8,64,128]{2,1,0:T(8,128)(2,1)}), bf16[8,64,128]{2,1,0:T(8,128)(2,1)S(1)}, u32[]{:S(2)}, u32[]{:S(2)}) async-start(bf16[8,64,128]{2,1,0:T(8,128)(2,1)} %bitcast.78), calls=%async_computation.2 | async-start | bytes 262144 | tf_op jit(solution)/shard_map/all_to_all | solution.py:154
  129.7 0.7 copy.349
  130.4 5.9 %all-to-all-done.2 = bf16[8,64,128]{2,1,0:T(8,128)(2,1)S(1)} async-done(((bf16[8,64,128]{2,1,0:T(8,128)(2,1)}), bf16[8,64,128]{2,1,0:T(8,128)(2,1)S(1)}, u32[]{:S(2)}, u32[]{:S(2)}) %all-to-all-start.2) | async-done | bytes 131104 | tf_op jit(solution)/shard_map/all_to_all | solution.py:154
  136.3 3.4 %all-to-all-start.1 = ((bf16[8,64,128]{2,1,0:T(8,128)(2,1)}), bf16[8,64,128]{2,1,0:T(8,128)(2,1)S(1)}, u32[]{:S(2)}, u32[]{:S(2)}) async-start(bf16[8,64,128]{2,1,0:T(8,128)(2,1)} %bitcast.76), calls=%async_computation.1 | async-start | bytes 262144 | tf_op jit(solution)/shard_map/all_to_all | solution.py:153
  139.7 1.3 all_to_all.38
  140.9 5.2 %all-to-all-done.1 = bf16[8,64,128]{2,1,0:T(8,128)(2,1)S(1)} async-done(((bf16[8,64,128]{2,1,0:T(8,128)(2,1)}), bf16[8,64,128]{2,1,0:T(8,128)(2,1)S(1)}, u32[]{:S(2)}, u32[]{:S(2)}) %all-to-all-start.1) | async-done | bytes 131104 | tf_op jit(solution)/shard_map/all_to_all | solution.py:153
  146.2 3.6 %all-to-all-start = ((bf16[8,64,1024]{2,1,0:T(8,128)(2,1)}), bf16[8,64,1024]{2,1,0:T(8,128)(2,1)S(1)}, u32[]{:S(2)}, u32[]{:S(2)}) async-start(bf16[8,64,1024]{2,1,0:T(8,128)(2,1)} %all_to_all.38), calls=%async_computation | async-start | bytes 2097152 | tf_op jit(solution)/shard_map/all_to_all | solution.py:152
  149.7 0.7 copy_bitcast_fusion.5
  150.4 0.7 copy_bitcast_fusion.6
  151.1 12.1 %all-to-all-done = bf16[8,64,1024]{2,1,0:T(8,128)(2,1)S(1)} async-done(((bf16[8,64,1024]{2,1,0:T(8,128)(2,1)}), bf16[8,64,1024]{2,1,0:T(8,128)(2,1)S(1)}, u32[]{:S(2)}, u32[]{:S(2)}) %all-to-all-start) | async-done | bytes 1048608 | tf_op jit(solution)/shard_map/all_to_all | solution.py:152
  163.2 1.1 copy.396
  (156 shorter events, 26.3 us)
Async XLA Ops:
  2.4 1.4 copy-start.6
  2.4 25.1 %copy-start.3 = (s32[256,4]{0,1:T(4,128)S(1)}, s32[256,4]{0,1:T(4,128)}, u32[]{:S(2)}) copy-start(s32[256,4]{0,1:T(4,128)} %param.11) | copy-start | bytes 12292
  3.4 25.3 %copy-start = (bf16[512,1024]{1,0:T(8,128)(2,1)S(1)}, bf16[512,1024]{1,0:T(8,128)(2,1)}, u32[]{:S(2)}) copy-start(bf16[512,1024]{1,0:T(8,128)(2,1)} %param.7) | copy-start | bytes 3145732
  4.7 24.2 %copy-start.1 = (bf16[512,1024]{1,0:T(8,128)(2,1)S(1)}, bf16[512,1024]{1,0:T(8,128)(2,1)}, u32[]{:S(2)}) copy-start(bf16[512,1024]{1,0:T(8,128)(2,1)} %param.10) | copy-start | bytes 3145732
  5.4 25.4 %collective-permute-start = (bf16[128,256]{1,0:T(8,128)(2,1)}, bf16[128,256]{1,0:T(8,128)(2,1)}, u32[]{:S(2)}, u32[]{:S(2)}) collective-permute-start(bf16[128,256]{1,0:T(8,128)(2,1)} %bitcast.256), channel_id=1, source_target_pairs={{0,8},{8,16},{16,24},{24,32},{32,40},{40,48},{48,56},{56,64},{64,7... | collective-permute-start | bytes 196616 | tf_op jit(solution)/shard_map/ppermute | solution.py:17
  7.9 28.7 %collective-permute-start.1 = (bf16[128,256]{1,0:T(8,128)(2,1)}, bf16[128,256]{1,0:T(8,128)(2,1)}, u32[]{:S(2)}, u32[]{:S(2)}) collective-permute-start(bf16[128,256]{1,0:T(8,128)(2,1)} %bitcast.255), channel_id=1, source_target_pairs={{0,16},{8,24},{16,32},{24,40},{32,48},{40,56},{48,64},{56,72},{64,... | collective-permute-start | bytes 196616 | tf_op jit(solution)/shard_map/ppermute | solution.py:17
  13.7 33.0 %collective-permute-start.2 = (bf16[128,256]{1,0:T(8,128)(2,1)}, bf16[128,256]{1,0:T(8,128)(2,1)}, u32[]{:S(2)}, u32[]{:S(2)}) collective-permute-start(bf16[128,256]{1,0:T(8,128)(2,1)} %bitcast.254), channel_id=1, source_target_pairs={{0,24},{8,32},{16,40},{24,48},{32,56},{40,64},{48,72},{56,80},{64,... | collective-permute-start | bytes 196616 | tf_op jit(solution)/shard_map/ppermute | solution.py:17
  19.9 31.0 %collective-permute-start.3 = (bf16[128,256]{1,0:T(8,128)(2,1)S(1)}, bf16[128,256]{1,0:T(8,128)(2,1)}, u32[]{:S(2)}, u32[]{:S(2)}) collective-permute-start(bf16[128,256]{1,0:T(8,128)(2,1)S(1)} %bitcast.319), channel_id=1, source_target_pairs={{0,32},{8,40},{16,48},{24,56},{32,64},{40,72},{48,80},{56,88},{64,... | collective-permute-start | bytes 196616 | tf_op jit(solution)/shard_map/ppermute | solution.py:17
  25.0 26.8 %collective-permute-start.4 = (bf16[128,256]{1,0:T(8,128)(2,1)S(1)}, bf16[128,256]{1,0:T(8,128)(2,1)}, u32[]{:S(2)}, u32[]{:S(2)}) collective-permute-start(bf16[128,256]{1,0:T(8,128)(2,1)S(1)} %bitcast.318), channel_id=1, source_target_pairs={{0,40},{8,48},{16,56},{24,64},{32,72},{40,80},{48,88},{56,96},{64,... | collective-permute-start | bytes 196616 | tf_op jit(solution)/shard_map/ppermute | solution.py:17
  27.7 0.8 copy-start.4
  30.2 24.3 %copy-start.9 = (pred[4,4]{1,0:T(4,128)(4,1)S(1)}, pred[4,4]{1,0:T(4,128)(4,1)}, u32[]{:S(2)}) copy-start(pred[4,4]{1,0:T(4,128)(4,1)} %copy.327) | copy-start | bytes 52
  30.8 21.8 %collective-permute-start.5 = (bf16[128,256]{1,0:T(8,128)(2,1)S(1)}, bf16[128,256]{1,0:T(8,128)(2,1)S(1)}, u32[]{:S(2)}, u32[]{:S(2)}) collective-permute-start(bf16[128,256]{1,0:T(8,128)(2,1)S(1)} %bitcast.330), channel_id=1, source_target_pairs={{0,48},{8,56},{16,64},{24,72},{32,80},{40,88},{48,96},{56,104},{64... | collective-permute-start | bytes 196616 | tf_op jit(solution)/shard_map/ppermute | solution.py:17
  36.6 16.0 %collective-permute-start.6 = (bf16[128,256]{1,0:T(8,128)(2,1)S(1)}, bf16[128,256]{1,0:T(8,128)(2,1)S(1)}, u32[]{:S(2)}, u32[]{:S(2)}) collective-permute-start(bf16[128,256]{1,0:T(8,128)(2,1)S(1)} %bitcast.324), channel_id=1, source_target_pairs={{0,56},{8,64},{16,72},{24,80},{32,88},{40,96},{48,104},{56,112},{6... | collective-permute-start | bytes 196616 | tf_op jit(solution)/shard_map/ppermute | solution.py:17
  46.7 7.1 %collective-permute-start.7 = (bf16[128,256]{1,0:T(8,128)(2,1)S(1)}, bf16[128,256]{1,0:T(8,128)(2,1)S(1)}, u32[]{:S(2)}, u32[]{:S(2)}) collective-permute-start(bf16[128,256]{1,0:T(8,128)(2,1)S(1)} %bitcast.321), channel_id=1, source_target_pairs={{0,64},{8,72},{16,80},{24,88},{32,96},{40,104},{48,112},{56,120},{... | collective-permute-start | bytes 196616 | tf_op jit(solution)/shard_map/ppermute | solution.py:17
  53.9 0.8 copy-start.10
  87.4 2.2 %copy-start.8 = (s32[8]{0:T(128)S(1)}, s32[8]{0:T(128)}, u32[]{:S(2)}) copy-start(s32[8]{0:T(128)} %iota_add_fusion.1) | copy-start | bytes 100
  89.7 10.9 %copy-start.5 = (s32[16]{0:T(128)S(1)}, s32[16]{0:T(128)}, u32[]{:S(2)}) copy-start(s32[16]{0:T(128)} %copy-done.4) | copy-start | bytes 196
  91.5 13.2 %collective-permute-start.8 = (bf16[128,256]{1,0:T(8,128)(2,1)S(1)}, bf16[128,256]{1,0:T(8,128)(2,1)S(1)}, u32[]{:S(2)}, u32[]{:S(2)}) collective-permute-start(bf16[128,256]{1,0:T(8,128)(2,1)S(1)} %bitcast.338), channel_id=1, source_target_pairs={{8,0},{16,8},{24,16},{32,24},{40,32},{48,40},{56,48},{64,56},{72,6... | collective-permute-start | bytes 196616 | tf_op jit(solution)/shard_map/ppermute | solution.py:17
  93.4 13.2 %collective-permute-start.9 = (bf16[128,256]{1,0:T(8,128)(2,1)S(1)}, bf16[128,256]{1,0:T(8,128)(2,1)S(1)}, u32[]{:S(2)}, u32[]{:S(2)}) collective-permute-start(bf16[128,256]{1,0:T(8,128)(2,1)S(1)} %bitcast.332), channel_id=1, source_target_pairs={{16,0},{24,8},{32,16},{40,24},{48,32},{56,40},{64,48},{72,56},{80,... | collective-permute-start | bytes 196616 | tf_op jit(solution)/shard_map/ppermute | solution.py:17
  97.8 10.8 %collective-permute-start.10 = (bf16[128,256]{1,0:T(8,128)(2,1)S(1)}, bf16[128,256]{1,0:T(8,128)(2,1)S(1)}, u32[]{:S(2)}, u32[]{:S(2)}) collective-permute-start(bf16[128,256]{1,0:T(8,128)(2,1)S(1)} %bitcast.328), channel_id=1, source_target_pairs={{24,0},{32,8},{40,16},{48,24},{56,32},{64,40},{72,48},{80,56},{88,... | collective-permute-start | bytes 196616 | tf_op jit(solution)/shard_map/ppermute | solution.py:17
  100.7 11.2 %collective-permute-start.11 = (bf16[128,256]{1,0:T(8,128)(2,1)S(1)}, bf16[128,256]{1,0:T(8,128)(2,1)S(1)}, u32[]{:S(2)}, u32[]{:S(2)}) collective-permute-start(bf16[128,256]{1,0:T(8,128)(2,1)S(1)} %bitcast.333), channel_id=1, source_target_pairs={{32,0},{40,8},{48,16},{56,24},{64,32},{72,40},{80,48},{88,56},{96,... | collective-permute-start | bytes 196616 | tf_op jit(solution)/shard_map/ppermute | solution.py:17
  102.8 9.2 %collective-permute-start.12 = (bf16[128,256]{1,0:T(8,128)(2,1)S(1)}, bf16[128,256]{1,0:T(8,128)(2,1)S(1)}, u32[]{:S(2)}, u32[]{:S(2)}) collective-permute-start(bf16[128,256]{1,0:T(8,128)(2,1)S(1)} %bitcast.329), channel_id=1, source_target_pairs={{40,0},{48,8},{56,16},{64,24},{72,32},{80,40},{88,48},{96,56},{104... | collective-permute-start | bytes 196616 | tf_op jit(solution)/shard_map/ppermute | solution.py:17
  104.7 8.6 %collective-permute-start.13 = (bf16[128,256]{1,0:T(8,128)(2,1)S(1)}, bf16[128,256]{1,0:T(8,128)(2,1)S(1)}, u32[]{:S(2)}, u32[]{:S(2)}) collective-permute-start(bf16[128,256]{1,0:T(8,128)(2,1)S(1)} %bitcast.323), channel_id=1, source_target_pairs={{48,0},{56,8},{64,16},{72,24},{80,32},{88,40},{96,48},{104,56},{11... | collective-permute-start | bytes 196616 | tf_op jit(solution)/shard_map/ppermute | solution.py:17
  106.7 8.1 %collective-permute-start.14 = (bf16[128,256]{1,0:T(8,128)(2,1)S(1)}, bf16[128,256]{1,0:T(8,128)(2,1)S(1)}, u32[]{:S(2)}, u32[]{:S(2)}) collective-permute-start(bf16[128,256]{1,0:T(8,128)(2,1)S(1)} %bitcast.322), channel_id=1, source_target_pairs={{56,0},{64,8},{72,16},{80,24},{88,32},{96,40},{104,48},{112,56},{1... | collective-permute-start | bytes 196616 | tf_op jit(solution)/shard_map/ppermute | solution.py:17
  108.6 13.9 %collective-permute-start.15 = (bf16[128,256]{1,0:T(8,128)(2,1)S(1)}, bf16[128,256]{1,0:T(8,128)(2,1)S(1)}, u32[]{:S(2)}, u32[]{:S(2)}) collective-permute-start(bf16[128,256]{1,0:T(8,128)(2,1)S(1)} %bitcast.320), channel_id=1, source_target_pairs={{64,0},{72,8},{80,16},{88,24},{96,32},{104,40},{112,48},{120,56},{... | collective-permute-start | bytes 196616 | tf_op jit(solution)/shard_map/ppermute | solution.py:17
  111.6 12.7 %copy-start.7 = (s32[8]{0:T(128)S(1)}, s32[8]{0:T(128)}, u32[]{:S(2)}) copy-start(s32[8]{0:T(128)} %copy-done.6) | copy-start | bytes 100
  122.6 17.0 %copy-start.2 = (bf16[4,1,128,1,8,128]{5,4,2,0,3,1:T(8,128)(2,1)S(1)}, bf16[4,1,128,1,8,128]{5,4,2,0,3,1:T(8,128)(2,1)}, u32[]{:S(2)}) copy-start(bf16[4,1,128,1,8,128]{5,4,2,0,3,1:T(8,128)(2,1)} %get-tuple-element.46) | copy-start | bytes 3145732
  125.3 11.0 %all-to-all-start.2 = ((bf16[8,64,128]{2,1,0:T(8,128)(2,1)}), bf16[8,64,128]{2,1,0:T(8,128)(2,1)S(1)}, u32[]{:S(2)}, u32[]{:S(2)}) async-start(bf16[8,64,128]{2,1,0:T(8,128)(2,1)} %bitcast.78), calls=%async_computation.2 | async-start | bytes 262144 | tf_op jit(solution)/shard_map/all_to_all | solution.py:154
  136.3 9.9 %all-to-all-start.1 = ((bf16[8,64,128]{2,1,0:T(8,128)(2,1)}), bf16[8,64,128]{2,1,0:T(8,128)(2,1)S(1)}, u32[]{:S(2)}, u32[]{:S(2)}) async-start(bf16[8,64,128]{2,1,0:T(8,128)(2,1)} %bitcast.76), calls=%async_computation.1 | async-start | bytes 262144 | tf_op jit(solution)/shard_map/all_to_all | solution.py:153
  146.2 17.0 %all-to-all-start = ((bf16[8,64,1024]{2,1,0:T(8,128)(2,1)}), bf16[8,64,1024]{2,1,0:T(8,128)(2,1)S(1)}, u32[]{:S(2)}, u32[]{:S(2)}) async-start(bf16[8,64,1024]{2,1,0:T(8,128)(2,1)} %all_to_all.38), calls=%async_computation | async-start | bytes 2097152 | tf_op jit(solution)/shard_map/all_to_all | solution.py:152
where the time goes:
time: 165 us; the launch traced here: 164 us
  starting transfers between devices  68 us (41%)
  waiting for transfers between devices  34.6 us (21%)
  local copies, waits for them, and re-layouts  33.6 us (20%)
  matrix products  14.5 us (9%)
  other arithmetic  11.8 us (7%)
    ppermute x16, starting transfers between devices, from_behind(): return lax.ppermute(x, axis, pairs)  56.7 us
    all_to_all x1, waiting for transfers between devices, body(): lax.all_to_all(query_local, 'head', split_axis=0, concat_axis=1, tiled=True)  12.1 us
    ppermute x16, waiting for transfers between devices, from_behind(): return lax.ppermute(x, axis, pairs)  11.4 us
    unnamed x49, local copies, waits for them, and re-layouts  8.68 us
    dynamic_slice x12, local copies, waits for them, and re-layouts, body(): lax.map(one_step, (query_steps, grad_steps, kv_steps, entry_steps, block_...  7.2 us
    all_to_all x1, waiting for transfers between devices, body(): lax.all_to_all(value_local, 'head', split_axis=0, concat_axis=1, tiled=True)  5.91 us
    all_to_all x1, waiting for transfers between devices, body(): lax.all_to_all(key_local, 'head', split_axis=0, concat_axis=1, tiled=True)  5.24 us
    all_to_all x1, starting transfers between devices, body(): lax.all_to_all(value_local, 'head', split_axis=0, concat_axis=1, tiled=True)  4.37 us
  transfers between devices with their start and end apart: 19, of which 7 were waited for; matrix products, arithmetic and copies ran while one was open for 8% of the time, Pallas kernels for 0%

commit v1 on v0

--- a/solution.py
+++ b/solution.py
@@ -9,6 +9,12 @@
 HEAD_DIM = 128
 BLOCK = 128
 REACH = 8
+
+
+def swap_blocks(x, mesh_axis, split, join):
+    pieces = jnp.split(x, lax.axis_size(mesh_axis), axis=split)
+    received = lax.all_to_all(jnp.stack(pieces), mesh_axis, 0, 0)
+    return jnp.concatenate(received, axis=join)
 
 
 def from_behind(x, axis, by):
@@ -151,7 +157,7 @@
     query_grad, key_grad, value_grad = (
         lax.all_to_all(query_local, "head", split_axis=0, concat_axis=1, tiled=True),
         lax.all_to_all(key_local, "head", split_axis=0, concat_axis=1, tiled=True),
-        lax.all_to_all(value_local, "head", split_axis=0, concat_axis=1, tiled=True),
+        swap_blocks(value_local, "head", 0, 1),
     )
     return (query_grad, key_grad, value_grad)
 

time: 165 us -> 170 us (1.030)
  local copies, waits for them, and re-layouts: 33.6 us -> 37.7 us
    unnamed x49 -> x54, local copies, waits for them, and re-layouts: 8.68 us -> 12.9 us
where the time goes in v1:
time: 170 us; the launch traced here: 169 us
  starting transfers between devices  68 us (40%)
  local copies, waits for them, and re-layouts  37.7 us (22%)
  waiting for transfers between devices  34.6 us (20%)
  matrix products  14.5 us (9%)
  other arithmetic  12.4 us (7%)
    ppermute x16, starting transfers between devices, from_behind(): return lax.ppermute(x, axis, pairs)  56.7 us
    unnamed x54, local copies, waits for them, and re-layouts  12.9 us
    all_to_all x1, waiting for transfers between devices, body(): lax.all_to_all(query_local, 'head', split_axis=0, concat_axis=1, tiled=True)  12.1 us
    ppermute x16, waiting for transfers between devices, from_behind(): return lax.ppermute(x, axis, pairs)  11.4 us
    dynamic_slice x12, local copies, waits for them, and re-layouts, body(): lax.map(one_step, (query_steps, grad_steps, kv_steps, entry_steps, block_...  7.2 us
    all_to_all x1, waiting for transfers between devices, swap_blocks(): received = lax.all_to_all(jnp.stack(pieces), mesh_axis, 0, 0)  5.91 us
    all_to_all x1, waiting for transfers between devices, body(): lax.all_to_all(key_local, 'head', split_axis=0, concat_axis=1, tiled=True)  5.24 us
    all_to_all x1, starting transfers between devices, swap_blocks(): received = lax.all_to_all(jnp.stack(pieces), mesh_axis, 0, 0)  4.4 us
  transfers between devices with their start and end apart: 19, of which 7 were waited for; matrix products, arithmetic and copies ran while one was open for 8% of the time, Pallas kernels for 0%

profile of v1, /device:TPU:64, one launch (start us, length us, event | category | flops | bytes accessed | tf_op | source)
XLA Modules:
  0.0 168.9 jit_solution(11867885658273465143)
XLA Ops:
  0.7 0.8 copy.335
  2.4 1.0 pad_maximum_fusion
  3.8 0.9 fusion.55
  5.3 1.9 %collective-permute-start = (bf16[128,256]{1,0:T(8,128)(2,1)}, bf16[128,256]{1,0:T(8,128)(2,1)}, u32[]{:S(2)}, u32[]{:S(2)}) collective-permute-start(bf16[128,256]{1,0:T(8,128)(2,1)} %bitcast.288), channel_id=1, source_target_pairs={{0,8},{8,16},{16,24},{24,32},{32,40},{40,48},{48,56},{56,64},{64,7... | collective-permute-start | bytes 196616 | tf_op jit(solution)/shard_map/ppermute | solution.py:23
  7.9 5.1 %collective-permute-start.1 = (bf16[128,256]{1,0:T(8,128)(2,1)}, bf16[128,256]{1,0:T(8,128)(2,1)}, u32[]{:S(2)}, u32[]{:S(2)}) collective-permute-start(bf16[128,256]{1,0:T(8,128)(2,1)} %bitcast.287), channel_id=1, source_target_pairs={{0,16},{8,24},{16,32},{24,40},{32,48},{40,56},{48,64},{56,72},{64,... | collective-permute-start | bytes 196616 | tf_op jit(solution)/shard_map/ppermute | solution.py:23
  13.6 6.2 %collective-permute-start.2 = (bf16[128,256]{1,0:T(8,128)(2,1)}, bf16[128,256]{1,0:T(8,128)(2,1)}, u32[]{:S(2)}, u32[]{:S(2)}) collective-permute-start(bf16[128,256]{1,0:T(8,128)(2,1)} %bitcast.286), channel_id=1, source_target_pairs={{0,24},{8,32},{16,40},{24,48},{32,56},{40,64},{48,72},{56,80},{64,... | collective-permute-start | bytes 196616 | tf_op jit(solution)/shard_map/ppermute | solution.py:23
  19.8 5.0 %collective-permute-start.3 = (bf16[128,256]{1,0:T(8,128)(2,1)S(1)}, bf16[128,256]{1,0:T(8,128)(2,1)}, u32[]{:S(2)}, u32[]{:S(2)}) collective-permute-start(bf16[128,256]{1,0:T(8,128)(2,1)S(1)} %bitcast.359), channel_id=1, source_target_pairs={{0,32},{8,40},{16,48},{24,56},{32,64},{40,72},{48,80},{56,88},{64,... | collective-permute-start | bytes 196616 | tf_op jit(solution)/shard_map/ppermute | solution.py:23
  24.9 1.9 %collective-permute-start.4 = (bf16[128,256]{1,0:T(8,128)(2,1)S(1)}, bf16[128,256]{1,0:T(8,128)(2,1)}, u32[]{:S(2)}, u32[]{:S(2)}) collective-permute-start(bf16[128,256]{1,0:T(8,128)(2,1)S(1)} %bitcast.358), channel_id=1, source_target_pairs={{0,40},{8,48},{16,56},{24,64},{32,72},{40,80},{48,88},{56,96},{64,... | collective-permute-start | bytes 196616 | tf_op jit(solution)/shard_map/ppermute | solution.py:23
  27.7 0.7 copy.334
  28.9 1.3 copy.407
  30.7 4.9 %collective-permute-start.5 = (bf16[128,256]{1,0:T(8,128)(2,1)S(1)}, bf16[128,256]{1,0:T(8,128)(2,1)S(1)}, u32[]{:S(2)}, u32[]{:S(2)}) collective-permute-start(bf16[128,256]{1,0:T(8,128)(2,1)S(1)} %bitcast.370), channel_id=1, source_target_pairs={{0,48},{8,56},{16,64},{24,72},{32,80},{40,88},{48,96},{56,104},{64... | collective-permute-start | bytes 196616 | tf_op jit(solution)/shard_map/ppermute | solution.py:23
  35.7 0.8 bitcast_dynamic-update-slice_fusion.7
  36.5 9.2 %collective-permute-start.6 = (bf16[128,256]{1,0:T(8,128)(2,1)S(1)}, bf16[128,256]{1,0:T(8,128)(2,1)S(1)}, u32[]{:S(2)}, u32[]{:S(2)}) collective-permute-start(bf16[128,256]{1,0:T(8,128)(2,1)S(1)} %bitcast.364), channel_id=1, source_target_pairs={{0,56},{8,64},{16,72},{24,80},{32,88},{40,96},{48,104},{56,112},{6... | collective-permute-start | bytes 196616 | tf_op jit(solution)/shard_map/ppermute | solution.py:23
  45.8 0.8 bitcast_dynamic-update-slice_fusion.6
  46.6 3.4 %collective-permute-start.7 = (bf16[128,256]{1,0:T(8,128)(2,1)S(1)}, bf16[128,256]{1,0:T(8,128)(2,1)S(1)}, u32[]{:S(2)}, u32[]{:S(2)}) collective-permute-start(bf16[128,256]{1,0:T(8,128)(2,1)S(1)} %bitcast.361), channel_id=1, source_target_pairs={{0,64},{8,72},{16,80},{24,88},{32,96},{40,104},{48,112},{56,120},{... | collective-permute-start | bytes 196616 | tf_op jit(solution)/shard_map/ppermute | solution.py:23
  50.0 0.8 bitcast_dynamic-update-slice_fusion.5
  50.9 0.8 bitcast_dynamic-update-slice_fusion.4
  51.7 0.8 bitcast_dynamic-update-slice_fusion.3
  52.6 1.2 collective-permute-done.7
  54.4 0.8 broadcast_select_fusion
  55.3 32.7 %while.12 = (s32[]{:T(128)}, bf16[4,1,128,1,8,128]{5,4,2,0,3,1:T(8,128)(2,1)}, f32[4,1,4,128,256]{3,4,2,1,0:T(8,128)}, bf16[4,1,4,128,256]{4,3,2,1,0:T(8,128)(2,...) while((s32[]{:T(128)}, ...), condition=%wide.region_6.7_spmd, body=%wide.region_1.6_spmd.sunk | while | flops 815806528 | bytes 21442768 | solution.py:136
  56.9 1.0 constant_dynamic-slice_fusion.8
  60.1 0.7 fusion.85
  61.9 0.7 constant_dynamic-update-slice_fusion.11
  62.6 0.8 fusion.87
  65.1 1.0 constant_dynamic-slice_fusion.8
  68.3 0.7 fusion.85
  70.0 0.7 constant_dynamic-update-slice_fusion.11
  70.8 0.8 fusion.87
  73.2 1.0 constant_dynamic-slice_fusion.8
  76.4 0.7 fusion.85
  78.2 0.7 constant_dynamic-update-slice_fusion.11
  78.9 0.9 fusion.87
  81.4 1.0 constant_dynamic-slice_fusion.8
  84.6 0.7 fusion.85
  86.4 0.7 constant_dynamic-update-slice_fusion.11
  87.1 0.8 fusion.87
  88.0 2.2 %copy.346 = f32[16,128,256]{2,0,1:T(8,128)S(1)} copy(f32[16,128,256]{1,2,0:T(8,128)} %bitcast.345) | data formatting | bytes 4194304 | tf_op jit(solution)/shard_map/reshape | solution.py:140
  90.2 0.8 convolution_convert_fusion.1
  91.1 0.9 fusion.54
  92.0 1.9 %collective-permute-start.8 = (bf16[128,256]{1,0:T(8,128)(2,1)S(1)}, bf16[128,256]{1,0:T(8,128)(2,1)S(1)}, u32[]{:S(2)}, u32[]{:S(2)}) collective-permute-start(bf16[128,256]{1,0:T(8,128)(2,1)S(1)} %bitcast.378), channel_id=1, source_target_pairs={{8,0},{16,8},{24,16},{32,24},{40,32},{48,40},{56,48},{64,56},{72,6... | collective-permute-start | bytes 196616 | tf_op jit(solution)/shard_map/ppermute | solution.py:23
  93.9 4.4 %collective-permute-start.9 = (bf16[128,256]{1,0:T(8,128)(2,1)S(1)}, bf16[128,256]{1,0:T(8,128)(2,1)S(1)}, u32[]{:S(2)}, u32[]{:S(2)}) collective-permute-start(bf16[128,256]{1,0:T(8,128)(2,1)S(1)} %bitcast.372), channel_id=1, source_target_pairs={{16,0},{24,8},{32,16},{40,24},{48,32},{56,40},{64,48},{72,56},{80,... | collective-permute-start | bytes 196616 | tf_op jit(solution)/shard_map/ppermute | solution.py:23
  98.3 2.7 %collective-permute-start.10 = (bf16[128,256]{1,0:T(8,128)(2,1)S(1)}, bf16[128,256]{1,0:T(8,128)(2,1)S(1)}, u32[]{:S(2)}, u32[]{:S(2)}) collective-permute-start(bf16[128,256]{1,0:T(8,128)(2,1)S(1)} %bitcast.368), channel_id=1, source_target_pairs={{24,0},{32,8},{40,16},{48,24},{56,32},{64,40},{72,48},{80,56},{88,... | collective-permute-start | bytes 196616 | tf_op jit(solution)/shard_map/ppermute | solution.py:23
  101.2 2.1 %collective-permute-start.11 = (bf16[128,256]{1,0:T(8,128)(2,1)S(1)}, bf16[128,256]{1,0:T(8,128)(2,1)S(1)}, u32[]{:S(2)}, u32[]{:S(2)}) collective-permute-start(bf16[128,256]{1,0:T(8,128)(2,1)S(1)} %bitcast.373), channel_id=1, source_target_pairs={{32,0},{40,8},{48,16},{56,24},{64,32},{72,40},{80,48},{88,56},{96,... | collective-permute-start | bytes 196616 | tf_op jit(solution)/shard_map/ppermute | solution.py:23
  103.3 1.9 %collective-permute-start.12 = (bf16[128,256]{1,0:T(8,128)(2,1)S(1)}, bf16[128,256]{1,0:T(8,128)(2,1)S(1)}, u32[]{:S(2)}, u32[]{:S(2)}) collective-permute-start(bf16[128,256]{1,0:T(8,128)(2,1)S(1)} %bitcast.369), channel_id=1, source_target_pairs={{40,0},{48,8},{56,16},{64,24},{72,32},{80,40},{88,48},{96,56},{104... | collective-permute-start | bytes 196616 | tf_op jit(solution)/shard_map/ppermute | solution.py:23
  105.2 1.9 %collective-permute-start.13 = (bf16[128,256]{1,0:T(8,128)(2,1)S(1)}, bf16[128,256]{1,0:T(8,128)(2,1)S(1)}, u32[]{:S(2)}, u32[]{:S(2)}) collective-permute-start(bf16[128,256]{1,0:T(8,128)(2,1)S(1)} %bitcast.363), channel_id=1, source_target_pairs={{48,0},{56,8},{64,16},{72,24},{80,32},{88,40},{96,48},{104,56},{11... | collective-permute-start | bytes 196616 | tf_op jit(solution)/shard_map/ppermute | solution.py:23
  107.1 1.9 %collective-permute-start.14 = (bf16[128,256]{1,0:T(8,128)(2,1)S(1)}, bf16[128,256]{1,0:T(8,128)(2,1)S(1)}, u32[]{:S(2)}, u32[]{:S(2)}) collective-permute-start(bf16[128,256]{1,0:T(8,128)(2,1)S(1)} %bitcast.362), channel_id=1, source_target_pairs={{56,0},{64,8},{72,16},{80,24},{88,32},{96,40},{104,48},{112,56},{1... | collective-permute-start | bytes 196616 | tf_op jit(solution)/shard_map/ppermute | solution.py:23
  109.1 2.1 %collective-permute-start.15 = (bf16[128,256]{1,0:T(8,128)(2,1)S(1)}, bf16[128,256]{1,0:T(8,128)(2,1)S(1)}, u32[]{:S(2)}, u32[]{:S(2)}) collective-permute-start(bf16[128,256]{1,0:T(8,128)(2,1)S(1)} %bitcast.360), channel_id=1, source_target_pairs={{64,0},{72,8},{80,16},{88,24},{96,32},{104,40},{112,48},{120,56},{... | collective-permute-start | bytes 196616 | tf_op jit(solution)/shard_map/ppermute | solution.py:23
  111.2 0.8 fusion.39
  112.6 1.1 collective-permute-done.13
  113.9 1.4 collective-permute-done.14
  115.4 7.6 %collective-permute-done.15 = bf16[128,256]{1,0:T(8,128)(2,1)S(1)} collective-permute-done((bf16[128,256]{1,0:T(8,128)(2,1)S(1)}, bf16[128,256]{1,0:T(8,128)(2,1)S(1)}, u32[]{:S(2)}, u32[]{:S(2)}) %collective-permute-start.15) | collective-permute-done | bytes 65568 | tf_op jit(solution)/shard_map/ppermute | solution.py:23
  123.1 1.6 stack.105
  130.0 4.4 %all-to-all-start.2 = ((bf16[8,64,128]{2,1,0:T(8,128)(2,1)}), bf16[8,64,128]{2,1,0:T(8,128)(2,1)S(1)}, u32[]{:S(2)}, u32[]{:S(2)}) async-start(bf16[8,64,128]{2,1,0:T(8,128)(2,1)} %constant_dynamic-update-slice_fusion.2), calls=%async_computation.2 | async-start | bytes 262144 | tf_op jit(solution)/shard_map/all_to_all | solution.py:16
  134.4 0.7 copy.356
  135.1 5.9 %all-to-all-done.2 = bf16[8,64,128]{2,1,0:T(8,128)(2,1)S(1)} async-done(((bf16[8,64,128]{2,1,0:T(8,128)(2,1)}), bf16[8,64,128]{2,1,0:T(8,128)(2,1)S(1)}, u32[]{:S(2)}, u32[]{:S(2)}) %all-to-all-start.2) | async-done | bytes 131104 | tf_op jit(solution)/shard_map/all_to_all | solution.py:16
  141.0 3.4 %all-to-all-start.1 = ((bf16[8,64,128]{2,1,0:T(8,128)(2,1)}), bf16[8,64,128]{2,1,0:T(8,128)(2,1)S(1)}, u32[]{:S(2)}, u32[]{:S(2)}) async-start(bf16[8,64,128]{2,1,0:T(8,128)(2,1)} %bitcast.76), calls=%async_computation.1 | async-start | bytes 262144 | tf_op jit(solution)/shard_map/all_to_all | solution.py:159
  144.4 1.3 all_to_all.29
  145.7 5.2 %all-to-all-done.1 = bf16[8,64,128]{2,1,0:T(8,128)(2,1)S(1)} async-done(((bf16[8,64,128]{2,1,0:T(8,128)(2,1)}), bf16[8,64,128]{2,1,0:T(8,128)(2,1)S(1)}, u32[]{:S(2)}, u32[]{:S(2)}) %all-to-all-start.1) | async-done | bytes 131104 | tf_op jit(solution)/shard_map/all_to_all | solution.py:159
  150.9 3.6 %all-to-all-start = ((bf16[8,64,1024]{2,1,0:T(8,128)(2,1)}), bf16[8,64,1024]{2,1,0:T(8,128)(2,1)S(1)}, u32[]{:S(2)}, u32[]{:S(2)}) async-start(bf16[8,64,1024]{2,1,0:T(8,128)(2,1)} %all_to_all.29), calls=%async_computation | async-start | bytes 2097152 | tf_op jit(solution)/shard_map/all_to_all | solution.py:158
  154.5 0.7 copy_bitcast_fusion.5
  155.1 0.7 copy_bitcast_fusion.6
  155.8 12.1 %all-to-all-done = bf16[8,64,1024]{2,1,0:T(8,128)(2,1)S(1)} async-done(((bf16[8,64,1024]{2,1,0:T(8,128)(2,1)}), bf16[8,64,1024]{2,1,0:T(8,128)(2,1)S(1)}, u32[]{:S(2)}, u32[]{:S(2)}) %all-to-all-start) | async-done | bytes 1048608 | tf_op jit(solution)/shard_map/all_to_all | solution.py:158
  167.9 1.1 copy.403
  (162 shorter events, 31.0 us)
Async XLA Ops:
  2.4 1.0 copy-start.6
  2.4 25.0 %copy-start.3 = (s32[256,4]{0,1:T(4,128)S(1)}, s32[256,4]{0,1:T(4,128)}, u32[]{:S(2)}) copy-start(s32[256,4]{0,1:T(4,128)} %param.11) | copy-start | bytes 12292
  3.4 25.2 %copy-start = (bf16[512,1024]{1,0:T(8,128)(2,1)S(1)}, bf16[512,1024]{1,0:T(8,128)(2,1)}, u32[]{:S(2)}) copy-start(bf16[512,1024]{1,0:T(8,128)(2,1)} %param.7) | copy-start | bytes 3145732
  4.7 24.2 %copy-start.1 = (bf16[512,1024]{1,0:T(8,128)(2,1)S(1)}, bf16[512,1024]{1,0:T(8,128)(2,1)}, u32[]{:S(2)}) copy-start(bf16[512,1024]{1,0:T(8,128)(2,1)} %param.10) | copy-start | bytes 3145732
  5.3 25.4 %collective-permute-start = (bf16[128,256]{1,0:T(8,128)(2,1)}, bf16[128,256]{1,0:T(8,128)(2,1)}, u32[]{:S(2)}, u32[]{:S(2)}) collective-permute-start(bf16[128,256]{1,0:T(8,128)(2,1)} %bitcast.288), channel_id=1, source_target_pairs={{0,8},{8,16},{16,24},{24,32},{32,40},{40,48},{48,56},{56,64},{64,7... | collective-permute-start | bytes 196616 | tf_op jit(solution)/shard_map/ppermute | solution.py:23
  7.9 28.7 %collective-permute-start.1 = (bf16[128,256]{1,0:T(8,128)(2,1)}, bf16[128,256]{1,0:T(8,128)(2,1)}, u32[]{:S(2)}, u32[]{:S(2)}) collective-permute-start(bf16[128,256]{1,0:T(8,128)(2,1)} %bitcast.287), channel_id=1, source_target_pairs={{0,16},{8,24},{16,32},{24,40},{32,48},{40,56},{48,64},{56,72},{64,... | collective-permute-start | bytes 196616 | tf_op jit(solution)/shard_map/ppermute | solution.py:23
  13.6 33.0 %collective-permute-start.2 = (bf16[128,256]{1,0:T(8,128)(2,1)}, bf16[128,256]{1,0:T(8,128)(2,1)}, u32[]{:S(2)}, u32[]{:S(2)}) collective-permute-start(bf16[128,256]{1,0:T(8,128)(2,1)} %bitcast.286), channel_id=1, source_target_pairs={{0,24},{8,32},{16,40},{24,48},{32,56},{40,64},{48,72},{56,80},{64,... | collective-permute-start | bytes 196616 | tf_op jit(solution)/shard_map/ppermute | solution.py:23
  19.8 31.0 %collective-permute-start.3 = (bf16[128,256]{1,0:T(8,128)(2,1)S(1)}, bf16[128,256]{1,0:T(8,128)(2,1)}, u32[]{:S(2)}, u32[]{:S(2)}) collective-permute-start(bf16[128,256]{1,0:T(8,128)(2,1)S(1)} %bitcast.359), channel_id=1, source_target_pairs={{0,32},{8,40},{16,48},{24,56},{32,64},{40,72},{48,80},{56,88},{64,... | collective-permute-start | bytes 196616 | tf_op jit(solution)/shard_map/ppermute | solution.py:23
  24.9 26.8 %collective-permute-start.4 = (bf16[128,256]{1,0:T(8,128)(2,1)S(1)}, bf16[128,256]{1,0:T(8,128)(2,1)}, u32[]{:S(2)}, u32[]{:S(2)}) collective-permute-start(bf16[128,256]{1,0:T(8,128)(2,1)S(1)} %bitcast.358), channel_id=1, source_target_pairs={{0,40},{8,48},{16,56},{24,64},{32,72},{40,80},{48,88},{56,96},{64,... | collective-permute-start | bytes 196616 | tf_op jit(solution)/shard_map/ppermute | solution.py:23
  27.7 0.8 copy-start.4
  30.7 21.8 %collective-permute-start.5 = (bf16[128,256]{1,0:T(8,128)(2,1)S(1)}, bf16[128,256]{1,0:T(8,128)(2,1)S(1)}, u32[]{:S(2)}, u32[]{:S(2)}) collective-permute-start(bf16[128,256]{1,0:T(8,128)(2,1)S(1)} %bitcast.370), channel_id=1, source_target_pairs={{0,48},{8,56},{16,64},{24,72},{32,80},{40,88},{48,96},{56,104},{64... | collective-permute-start | bytes 196616 | tf_op jit(solution)/shard_map/ppermute | solution.py:23
  36.5 16.0 %collective-permute-start.6 = (bf16[128,256]{1,0:T(8,128)(2,1)S(1)}, bf16[128,256]{1,0:T(8,128)(2,1)S(1)}, u32[]{:S(2)}, u32[]{:S(2)}) collective-permute-start(bf16[128,256]{1,0:T(8,128)(2,1)S(1)} %bitcast.364), channel_id=1, source_target_pairs={{0,56},{8,64},{16,72},{24,80},{32,88},{40,96},{48,104},{56,112},{6... | collective-permute-start | bytes 196616 | tf_op jit(solution)/shard_map/ppermute | solution.py:23
  46.6 7.2 %collective-permute-start.7 = (bf16[128,256]{1,0:T(8,128)(2,1)S(1)}, bf16[128,256]{1,0:T(8,128)(2,1)S(1)}, u32[]{:S(2)}, u32[]{:S(2)}) collective-permute-start(bf16[128,256]{1,0:T(8,128)(2,1)S(1)} %bitcast.361), channel_id=1, source_target_pairs={{0,64},{8,72},{16,80},{24,88},{32,96},{40,104},{48,112},{56,120},{... | collective-permute-start | bytes 196616 | tf_op jit(solution)/shard_map/ppermute | solution.py:23
  53.8 1.5 copy-start.9
  88.0 2.2 %copy-start.8 = (s32[8]{0:T(128)S(1)}, s32[8]{0:T(128)}, u32[]{:S(2)}) copy-start(s32[8]{0:T(128)} %iota_add_fusion.1) | copy-start | bytes 100
  90.2 10.8 %copy-start.5 = (s32[16]{0:T(128)S(1)}, s32[16]{0:T(128)}, u32[]{:S(2)}) copy-start(s32[16]{0:T(128)} %copy-done.4) | copy-start | bytes 196
  92.0 13.2 %collective-permute-start.8 = (bf16[128,256]{1,0:T(8,128)(2,1)S(1)}, bf16[128,256]{1,0:T(8,128)(2,1)S(1)}, u32[]{:S(2)}, u32[]{:S(2)}) collective-permute-start(bf16[128,256]{1,0:T(8,128)(2,1)S(1)} %bitcast.378), channel_id=1, source_target_pairs={{8,0},{16,8},{24,16},{32,24},{40,32},{48,40},{56,48},{64,56},{72,6... | collective-permute-start | bytes 196616 | tf_op jit(solution)/shard_map/ppermute | solution.py:23
  93.9 13.2 %collective-permute-start.9 = (bf16[128,256]{1,0:T(8,128)(2,1)S(1)}, bf16[128,256]{1,0:T(8,128)(2,1)S(1)}, u32[]{:S(2)}, u32[]{:S(2)}) collective-permute-start(bf16[128,256]{1,0:T(8,128)(2,1)S(1)} %bitcast.372), channel_id=1, source_target_pairs={{16,0},{24,8},{32,16},{40,24},{48,32},{56,40},{64,48},{72,56},{80,... | collective-permute-start | bytes 196616 | tf_op jit(solution)/shard_map/ppermute | solution.py:23
  98.3 10.8 %collective-permute-start.10 = (bf16[128,256]{1,0:T(8,128)(2,1)S(1)}, bf16[128,256]{1,0:T(8,128)(2,1)S(1)}, u32[]{:S(2)}, u32[]{:S(2)}) collective-permute-start(bf16[128,256]{1,0:T(8,128)(2,1)S(1)} %bitcast.368), channel_id=1, source_target_pairs={{24,0},{32,8},{40,16},{48,24},{56,32},{64,40},{72,48},{80,56},{88,... | collective-permute-start | bytes 196616 | tf_op jit(solution)/shard_map/ppermute | solution.py:23
  101.2 11.2 %collective-permute-start.11 = (bf16[128,256]{1,0:T(8,128)(2,1)S(1)}, bf16[128,256]{1,0:T(8,128)(2,1)S(1)}, u32[]{:S(2)}, u32[]{:S(2)}) collective-permute-start(bf16[128,256]{1,0:T(8,128)(2,1)S(1)} %bitcast.373), channel_id=1, source_target_pairs={{32,0},{40,8},{48,16},{56,24},{64,32},{72,40},{80,48},{88,56},{96,... | collective-permute-start | bytes 196616 | tf_op jit(solution)/shard_map/ppermute | solution.py:23
  103.3 9.2 %collective-permute-start.12 = (bf16[128,256]{1,0:T(8,128)(2,1)S(1)}, bf16[128,256]{1,0:T(8,128)(2,1)S(1)}, u32[]{:S(2)}, u32[]{:S(2)}) collective-permute-start(bf16[128,256]{1,0:T(8,128)(2,1)S(1)} %bitcast.369), channel_id=1, source_target_pairs={{40,0},{48,8},{56,16},{64,24},{72,32},{80,40},{88,48},{96,56},{104... | collective-permute-start | bytes 196616 | tf_op jit(solution)/shard_map/ppermute | solution.py:23
  105.2 8.6 %collective-permute-start.13 = (bf16[128,256]{1,0:T(8,128)(2,1)S(1)}, bf16[128,256]{1,0:T(8,128)(2,1)S(1)}, u32[]{:S(2)}, u32[]{:S(2)}) collective-permute-start(bf16[128,256]{1,0:T(8,128)(2,1)S(1)} %bitcast.363), channel_id=1, source_target_pairs={{48,0},{56,8},{64,16},{72,24},{80,32},{88,40},{96,48},{104,56},{11... | collective-permute-start | bytes 196616 | tf_op jit(solution)/shard_map/ppermute | solution.py:23
  107.1 8.1 %collective-permute-start.14 = (bf16[128,256]{1,0:T(8,128)(2,1)S(1)}, bf16[128,256]{1,0:T(8,128)(2,1)S(1)}, u32[]{:S(2)}, u32[]{:S(2)}) collective-permute-start(bf16[128,256]{1,0:T(8,128)(2,1)S(1)} %bitcast.362), channel_id=1, source_target_pairs={{56,0},{64,8},{72,16},{80,24},{88,32},{96,40},{104,48},{112,56},{1... | collective-permute-start | bytes 196616 | tf_op jit(solution)/shard_map/ppermute | solution.py:23
  109.1 13.9 %collective-permute-start.15 = (bf16[128,256]{1,0:T(8,128)(2,1)S(1)}, bf16[128,256]{1,0:T(8,128)(2,1)S(1)}, u32[]{:S(2)}, u32[]{:S(2)}) collective-permute-start(bf16[128,256]{1,0:T(8,128)(2,1)S(1)} %bitcast.360), channel_id=1, source_target_pairs={{64,0},{72,8},{80,16},{88,24},{96,32},{104,40},{112,48},{120,56},{... | collective-permute-start | bytes 196616 | tf_op jit(solution)/shard_map/ppermute | solution.py:23
  112.0 12.7 %copy-start.7 = (s32[8]{0:T(128)S(1)}, s32[8]{0:T(128)}, u32[]{:S(2)}) copy-start(s32[8]{0:T(128)} %copy-done.6) | copy-start | bytes 100
  123.1 21.3 %copy-start.2 = (bf16[4,1,128,1,8,128]{5,4,2,0,3,1:T(8,128)(2,1)S(1)}, bf16[4,1,128,1,8,128]{5,4,2,0,3,1:T(8,128)(2,1)}, u32[]{:S(2)}) copy-start(bf16[4,1,128,1,8,128]{5,4,2,0,3,1:T(8,128)(2,1)} %get-tuple-element.46) | copy-start | bytes 3145732
  130.0 11.0 %all-to-all-start.2 = ((bf16[8,64,128]{2,1,0:T(8,128)(2,1)}), bf16[8,64,128]{2,1,0:T(8,128)(2,1)S(1)}, u32[]{:S(2)}, u32[]{:S(2)}) async-start(bf16[8,64,128]{2,1,0:T(8,128)(2,1)} %constant_dynamic-update-slice_fusion.2), calls=%async_computation.2 | async-start | bytes 262144 | tf_op jit(solution)/shard_map/all_to_all | solution.py:16
  141.0 9.9 %all-to-all-start.1 = ((bf16[8,64,128]{2,1,0:T(8,128)(2,1)}), bf16[8,64,128]{2,1,0:T(8,128)(2,1)S(1)}, u32[]{:S(2)}, u32[]{:S(2)}) async-start(bf16[8,64,128]{2,1,0:T(8,128)(2,1)} %bitcast.76), calls=%async_computation.1 | async-start | bytes 262144 | tf_op jit(solution)/shard_map/all_to_all | solution.py:159
  150.9 17.0 %all-to-all-start = ((bf16[8,64,1024]{2,1,0:T(8,128)(2,1)}), bf16[8,64,1024]{2,1,0:T(8,128)(2,1)S(1)}, u32[]{:S(2)}, u32[]{:S(2)}) async-start(bf16[8,64,1024]{2,1,0:T(8,128)(2,1)} %all_to_all.29), calls=%async_computation | async-start | bytes 2097152 | tf_op jit(solution)/shard_map/all_to_all | solution.py:158
